TPU v7x, 512 devices: a whole 4x8x8 slice. The times are simulated.
512 devices in a mesh: tri: 32 (over y, z_lo), vir: 16 (over x, z_hi, core).
Axes of the slice: x: 4, y: 8, z: 8 (z_hi: 2, z_lo: 4; z = z_hi * 4 + z_lo), core: 2. Of those that a mesh axis runs over, the one named last changes fastest.
Arguments:
- amps: bfloat16 [96, 768, 768], P('tri', 'vir'), may hold values from -0.21875 to 0.21875
- vvvo: bfloat16 [96, 768, 128], P('tri', 'vir'), may hold values from -6 to 6
- occ_gap: float32 [64], replicated, may hold values from 0.3 to 1
- vir_gap: float32 [768], P('vir'), may hold values from 0.5 to 2
- pair_gap: float32 [128], replicated, may hold values from 0.5 to 2
- block_sizes: int32 [32], replicated, may hold values from 1 to 3, 64 in all
- roots: int32 [32], replicated, may hold values from 0 to 31, each once
- triples: int32 [384, 2], P('tri'), may hold values from 0 to 31
Outputs:
- density: float32 [768, 128], P('vir')
- grad: float32 [96, 768, 128], P('tri', 'vir')
Inputs may be any that keep to these rules, and one draw needn't show every extreme that they name: `block_sizes`: block sizes sum to 64; at least one block has exactly 3 orbitals. `roots`: each tri index stores exactly one block. `triples`: block numbers; a pair may repeat a block.
All inputs are finite; a program needn't handle non-finite values.
Results may differ from a plain program's by a relative error of at most 0.0003.
Values may be sent and summed in bfloat16 or wider, within the bound.
No kernel may reach another device: no remote copies, remote signals or barrier semaphores. Data moves between devices by JAX's collectives and lax.ppermute only.
A program may use at most 64 MiB of HBM per device.

v0:
```python
import jax
import jax.numpy as jnp
from jax import lax
from jax.sharding import PartitionSpec as P

BMAX = 3


def body(amps, vvvo, occ_gap, vir_gap, pair_gap, block_sizes, roots, triples):
    tri_count = lax.axis_size("tri")
    me = lax.axis_index("tri")
    npair = triples.shape[0]
    nocc = occ_gap.shape[0]
    nrow = tri_count * BMAX
    f32, bf16 = (jnp.float32, jnp.bfloat16)
    slots = jnp.arange(BMAX, dtype=jnp.int32)
    offsets = (jnp.cumsum(block_sizes) - block_sizes).astype(jnp.int32)
    own = roots == me
    own_size = jnp.sum(jnp.where(own, block_sizes, 0))
    own_off = jnp.sum(jnp.where(own, offsets, 0))
    own_gap = occ_gap[jnp.minimum(own_off + slots, nocc - 1)]
    own_live = slots < own_size
    pair_root = roots[triples]
    pair_gap_occ = occ_gap[jnp.minimum(offsets[triples][..., None] + slots, nocc - 1)]
    pair_live = slots < block_sizes[triples][..., None]
    rows = pair_root[..., None] * BMAX + slots
    everything = lax.all_gather(amps, "tri", axis=0, tiled=True)
    table = lax.all_gather(vvvo, "vir", axis=1, tiled=True)
    pick = (rows.reshape(-1)[:, None] == jnp.arange(nrow, dtype=jnp.int32)).astype(bf16)
    picked = jnp.einsum("rb,bad->rad", pick, everything, preferred_element_type=bf16)
    proj = jnp.einsum("rad,kdm->rakm", picked, table, preferred_element_type=f32)
    nv, nk, nm = (proj.shape[1], proj.shape[2], proj.shape[3])
    proj = proj.reshape(npair, 2, BMAX, nv, nk, nm)
    left, right = (proj[:, 0], proj[:, 1])
    base = vir_gap[:, None, None] + own_gap[None, :, None] + pair_gap[None, None, :]
    den = (
        base[None, None, None]
        + pair_gap_occ[:, 0, :, None, None, None, None]
        + pair_gap_occ[:, 1, None, :, None, None, None]
    )
    live = (
        pair_live[:, 0, :, None, None, None, None]
        & pair_live[:, 1, None, :, None, None, None]
        & own_live[None, None, None, None, :, None]
    )
    weighted = jnp.where(live, left[:, :, None] * right[:, None] / den, 0.0)
    dens_part = jnp.sum(weighted * weighted, axis=(0, 1, 2, 4))
    summed = jnp.sum(weighted, axis=2)
    hi_f32 = lax.reduce_precision(summed, exponent_bits=8, mantissa_bits=7)
    hi = hi_f32.astype(bf16)
    lo = (summed - hi_f32).astype(bf16)
    left_rows = picked.reshape(npair, 2, BMAX, nv, -1)[:, 0]
    grad = jnp.einsum("qiad,qiakm->dkm", left_rows, hi, preferred_element_type=f32)
    grad = grad + jnp.einsum("qiad,qiakm->dkm", left_rows, lo, preferred_element_type=f32)
    grad = lax.psum_scatter(grad, "vir", scatter_dimension=0, tiled=True)
    grad = jnp.transpose(grad, (1, 0, 2))
    density = lax.psum(dens_part, "tri") / float(tri_count * npair)
    return (density, grad)


def solution(mesh):
    return jax.shard_map(
        body,
        mesh=mesh,
        in_specs=(
            P("tri", "vir", None),
            P("tri", "vir", None),
            P(),
            P("vir"),
            P(),
            P(),
            P(),
            P("tri", None),
        ),
        out_specs=(P("vir", None), P("tri", "vir", None)),
        check_vma=False,
    )
```

profile of v0, /device:TPU:4, one launch (start us, length us, event | category | flops | bytes accessed | tf_op | source)
XLA Modules:
  0.0 373.6 jit_solution(18367673848902578636)
XLA Ops:
  7.2 0.7 all-gather.2.cloned.1.call-update
  7.9 0.0 reduce-scatter.2.cloned.1.call-start
  8.0 0.7 copy.60
  8.7 0.1 reduce-window.9
  8.8 0.1 reduce
  8.9 0.7 compare_select_fusion.1
  9.6 0.1 copy.54
  9.7 0.1 reshape.160
  9.8 0.7 gather_fusion
  10.5 0.7 gather_fusion.1
  11.2 0.6 fusion.17
  11.8 0.7 gather_fusion.3
  12.5 0.1 reshape.183
  12.6 0.1 compare_select_fusion
  12.7 0.1 reshape.192
  12.9 1.2 gather_fusion.4
  14.1 0.1 reshape.191
  14.2 0.1 copy.63
  14.3 0.1 copy.64
  14.4 0.1 copy.61
  14.5 0.1 copy.62
  14.6 0.7 fusion.19
  15.3 0.6 gather_fusion.2
  15.9 0.1 reshape.206
  16.0 0.1 iota_add_fusion
  16.1 0.1 add.157
  16.2 0.1 reshape.159
  16.3 0.1 copy.55
  16.4 0.1 copy.57
  16.5 0.1 copy.56
  16.6 0.7 iota_compare_fusion.2
  17.3 0.1 broadcast_add_fusion.2
  17.4 0.1 broadcast_and_fusion.1
  17.5 0.1 broadcast_and_fusion
  17.6 0.1 broadcast_add_fusion.1
  17.7 52.4 %all_gather.7 = bf16[3,768,128]{2,1,0:T(8,128)(2,1)S(1)} all-gather(bf16[3,48,128]{2,1,0:T(8,128)(2,1)S(1)} %copy-done.3), channel_id=1, replica_groups=mesh['tri'=32,'vir'=16] {'vir'}, dimensions={1}, use_global_device_ids=true | all-gather | bytes 626688 | tf_op jit(solution)/shard_map/all_gather | solution.py:28
  70.1 0.2 broadcast_add_fusion
  70.3 124.9 %all-gather.2.cloned.1.call-done = bf16[96,48,768]{2,1,0:T(8,128)(2,1)} async-done(((bf16[3,48,768]{2,1,0:T(8,128)(2,1)}), bf16[96,48,768]{2,1,0:T(8,128)(2,1)}) %all-gather.2.cloned.1.call-update) | async-done | bytes 7077904 | tf_op jit(solution)/shard_map/all_gather | solution.py:27
  195.3 7.9 %fusion = bf16[72,48,768]{2,0,1:T(8,128)(2,1)S(1)} fusion(bf16[96,48,768]{2,1,0:T(8,128)(2,1)} %all-gather.2.cloned.1.call-done, s32[72]{0:T(128)S(1)} %add.157), kind=kOutput, calls=%fused_computation.7 | convolution fusion | flops 509614848 | bytes 12386592 | tf_op jit(solution)/shard_map/rb,bad->rad/dot_general | solution.py:30
  203.2 1.0 copy.65
  204.3 2.9 fusion.3
  207.2 0.5 slice_bitcast_fusion.1
  207.7 3.1 fusion.2
  210.8 0.4 fusion.5
  211.2 1.6 fusion.8
  212.9 2.7 fusion.10
  215.5 150.6 %psum.7 = f32[48,128]{1,0:T(8,128)S(1)} all-reduce(f32[48,128]{1,0:T(8,128)S(1)} %get-tuple-element.3), channel_id=1, replica_groups=mesh['tri'=32,'vir'=16] {'tri'}, use_global_device_ids=true, to_apply=%region_4.5 | all-reduce | flops 6144 | bytes 49152 | tf_op jit(solution)/shard_map/psum | solution.py:57
  366.2 0.6 broadcast_multiply_fusion
  (22 shorter events, 0.1 us)
Async XLA Ops:
  7.2 5.7 %copy-start = (f32[64]{0:T(128)S(1)}, f32[64]{0:T(128)}, u32[]{:S(2)}) copy-start(f32[64]{0:T(128)} %param.10) | copy-start | bytes 772
  7.2 2.6 copy-start.1
  7.2 188.1 %all-gather.2.cloned.1.call-start = ((), (), s32[]{:S(2)}) async-start(), calls=%async_computation.1 | async-start | bytes 7299072 | tf_op jit(solution)/shard_map/all_gather | solution.py:27
  7.9 358.9 %reduce-scatter.2.cloned.1.call-start = ((), (), s32[]{:S(2)}) async-start(), calls=%async_computation.2 | async-start | bytes 1253376 | tf_op jit(solution)/shard_map/reduce_scatter | solution.py:55
  9.8 0.7 copy-start.2
  12.8 4.5 %copy-start.5 = (f32[48]{0:T(128)S(1)}, f32[48]{0:T(128)}, u32[]{:S(2)}) copy-start(f32[48]{0:T(128)} %param.11) | copy-start | bytes 580
  12.9 4.7 %copy-start.4 = (f32[128]{0:T(128)S(1)}, f32[128]{0:T(128)}, u32[]{:S(2)}) copy-start(f32[128]{0:T(128)} %param.12) | copy-start | bytes 1540
  12.9 4.8 %copy-start.3 = (bf16[3,48,128]{2,1,0:T(8,128)(2,1)S(1)}, bf16[3,48,128]{2,1,0:T(8,128)(2,1)}, u32[]{:S(2)}) copy-start(bf16[3,48,128]{2,1,0:T(8,128)(2,1)} %param.9) | copy-start | bytes 110596
Sparse Core Ops, SparseCore 0:
  10.1 185.1 all-gather.1
  215.7 86.1 reduce-scatter.1
where the time goes:
time: 374 us
  blocking collectives  203 us (54%)
  waiting for transfers between devices  126 us (34%)
  matrix products  15.1 us (4%)
  between operations  14.3 us (4%)
  other arithmetic  7.75 us (2%)
  local copies, waits for them, and re-layouts  7.68 us (2%)
    psum x1, blocking collectives, body(): density = lax.psum(dens_part, 'tri') / float(tri_count * npair)  151 us
    all_gather x1, waiting for transfers between devices, body(): everything = lax.all_gather(amps, 'tri', axis=0, tiled=True)  125 us
    all_gather x1, blocking collectives, body(): table = lax.all_gather(vvvo, 'vir', axis=1, tiled=True)  52.4 us
    dot_general x1, matrix products, body(): jnp.einsum('rb,bad->rad', pick, everything, preferred_element_type=bf16)  7.92 us
  transfers between devices with their start and end apart: 2, of which 1 were waited for; matrix products, arithmetic and copies ran while one was open for 3% of the time, Pallas kernels for 0%

commit v1 on v0

--- a/solution.py
+++ b/solution.py
@@ -54,7 +54,7 @@
     grad = grad + jnp.einsum("qiad,qiakm->dkm", left_rows, lo, preferred_element_type=f32)
     grad = lax.psum_scatter(grad, "vir", scatter_dimension=0, tiled=True)
     grad = jnp.transpose(grad, (1, 0, 2))
-    density = lax.psum(dens_part, "tri") / float(tri_count * npair)
+    density = jnp.sum(lax.all_gather(dens_part, "tri"), axis=0) / float(tri_count * npair)
     return (density, grad)
 
 

time: 374 us -> 312 us (0.83)
  the two profiles are of different devices: /device:TPU:4 before, /device:TPU:8 now
where the time goes in v1:
time: 312 us
  waiting for transfers between devices  134 us (43%)
  blocking collectives  133 us (43%)
  matrix products  15.1 us (5%)
  between operations  14.3 us (5%)
  other arithmetic  7.82 us (3%)
  local copies, waits for them, and re-layouts  7.68 us (2%)
    all_gather x1, waiting for transfers between devices, body(): everything = lax.all_gather(amps, 'tri', axis=0, tiled=True)  121 us
    all_gather x1, blocking collectives, body(): lax.all_gather(dens_part, 'tri')  77.7 us
    all_gather x1, blocking collectives, body(): table = lax.all_gather(vvvo, 'vir', axis=1, tiled=True)  54.9 us
    reduce_scatter x1, waiting for transfers between devices, body(): grad = lax.psum_scatter(grad, 'vir', scatter_dimension=0, tiled=True)  12.8 us
    dot_general x1, matrix products, body(): jnp.einsum('rb,bad->rad', pick, everything, preferred_element_type=bf16)  7.92 us
  transfers between devices with their start and end apart: 2, of which 2 were waited for; matrix products, arithmetic and copies ran while one was open for 3% of the time, Pallas kernels for 0%

profile of v1, /device:TPU:8, one launch (start us, length us, event | category | flops | bytes accessed | tf_op | source)
XLA Modules:
  0.0 312.1 jit_solution(5299012000034092142)
XLA Ops:
  7.2 0.7 all-gather.3.cloned.1.call-update
  8.0 0.7 copy.60
  8.8 0.1 reduce
  8.9 0.7 compare_select_fusion.1
  9.6 0.1 copy.54
  9.7 0.1 reshape.160
  9.8 0.7 gather_fusion
  10.5 0.7 gather_fusion.1
  11.2 0.6 fusion.17
  11.8 0.7 gather_fusion.3
  12.5 0.1 reshape.183
  12.6 0.1 compare_select_fusion
  12.7 0.1 reshape.192
  12.9 1.2 gather_fusion.4
  14.1 0.1 reshape.191
  14.2 0.1 copy.63
  14.3 0.1 copy.64
  14.4 0.1 copy.61
  14.5 0.1 copy.62
  14.6 0.7 fusion.19
  15.3 0.6 gather_fusion.2
  15.9 0.1 reshape.207
  16.0 0.1 iota_add_fusion
  16.1 0.1 add.155
  16.2 0.1 reshape.159
  16.3 0.1 copy.55
  16.4 0.1 copy.57
  16.5 0.1 copy.56
  16.6 0.7 iota_compare_fusion.2
  17.3 0.1 broadcast_add_fusion.2
  17.4 0.1 broadcast_and_fusion.1
  17.5 0.1 broadcast_and_fusion
  17.6 0.1 broadcast_add_fusion.1
  17.7 54.9 %all_gather.13 = bf16[3,768,128]{2,1,0:T(8,128)(2,1)S(1)} all-gather(bf16[3,48,128]{2,1,0:T(8,128)(2,1)S(1)} %copy-done.3), channel_id=1, replica_groups=mesh['tri'=32,'vir'=16] {'vir'}, dimensions={1}, use_global_device_ids=true | all-gather | bytes 626688 | tf_op jit(solution)/shard_map/all_gather | solution.py:28
  72.5 0.2 broadcast_add_fusion
  72.8 121.0 %all-gather.3.cloned.1.call-done = bf16[96,48,768]{2,1,0:T(8,128)(2,1)} async-done(((bf16[3,48,768]{2,1,0:T(8,128)(2,1)}), bf16[96,48,768]{2,1,0:T(8,128)(2,1)}) %all-gather.3.cloned.1.call-update) | async-done | bytes 7077904 | tf_op jit(solution)/shard_map/all_gather | solution.py:27
  193.8 7.9 %fusion = bf16[72,48,768]{2,0,1:T(8,128)(2,1)S(1)} fusion(bf16[96,48,768]{2,1,0:T(8,128)(2,1)} %all-gather.3.cloned.1.call-done, s32[72]{0:T(128)S(1)} %add.155), kind=kOutput, calls=%fused_computation.7 | convolution fusion | flops 509614848 | bytes 12386592 | tf_op jit(solution)/shard_map/rb,bad->rad/dot_general | solution.py:30
  201.7 1.0 copy.65
  202.7 2.9 fusion.3
  205.7 0.5 slice_bitcast_fusion.1
  206.1 3.1 %fusion.2 = (f32[12,3,48,3,128]{4,2,3,1,0:T(8,128)S(1)}, f32[48,128]{1,0:T(8,128)S(1)}) fusion(f32[12,3]{1,0:T(8,128)S(1)} %copy.64, f32[12,3,48,3,128]{4,2,3,1,0:T(8,128)S(1)} %broadcast_add_fusion, f32[12,3,48,3,128]{4,2,3,1,0:T(8,128)S(1)} %get-tuple-element.8, f32[12,3,48,3,128]{4,2,3,1,0:T(8,128)S(1)} %get-tuple-element.7, ...), kind=kLoop, calls=%fused_computation.9 | loop fusion | flops 13264896 | bytes 10641876 | tf_op jit(solution)/shard_map/reduce_sum | solution.py:48
  209.3 0.4 fusion.5
  209.7 1.6 fusion.8
  211.4 2.7 fusion.10
  214.0 77.7 %all-gather = f32[1536,128]{1,0:T(8,128)S(1)} all-gather(f32[48,128]{1,0:T(8,128)S(1)} %get-tuple-element.3), channel_id=2, replica_groups=mesh['tri'=32,'vir'=16] {'tri'}, dimensions={0}, use_global_device_ids=true | all-gather | bytes 811008 | tf_op jit(solution)/shard_map/all_gather | solution.py:57
  291.7 0.1 reduce_sum.48
  291.8 0.6 broadcast_multiply_fusion
  292.4 12.8 %reduce-scatter.2.cloned.1.call-done = f32[48,3,128]{2,0,1:T(8,128)} async-done(((f32[768,3,128]{2,0,1:T(8,128)}), f32[48,3,128]{2,0,1:T(8,128)}) %reduce-scatter.2.cloned.1.call-update) | async-done | bytes 73744 | tf_op jit(solution)/shard_map/reduce_scatter | solution.py:55
  (23 shorter events, 0.2 us)
Async XLA Ops:
  7.2 5.7 %copy-start = (f32[64]{0:T(128)S(1)}, f32[64]{0:T(128)}, u32[]{:S(2)}) copy-start(f32[64]{0:T(128)} %param.10) | copy-start | bytes 772
  7.2 2.6 copy-start.1
  7.2 186.6 %all-gather.3.cloned.1.call-start = ((), (), s32[]{:S(2)}) async-start(), calls=%async_computation.1 | async-start | bytes 7299072 | tf_op jit(solution)/shard_map/all_gather | solution.py:27
  7.9 297.3 %reduce-scatter.2.cloned.1.call-start = ((), (), s32[]{:S(2)}) async-start(), calls=%async_computation.2 | async-start | bytes 1253376 | tf_op jit(solution)/shard_map/reduce_scatter | solution.py:55
  9.8 0.7 copy-start.2
  12.8 4.5 %copy-start.5 = (f32[48]{0:T(128)S(1)}, f32[48]{0:T(128)}, u32[]{:S(2)}) copy-start(f32[48]{0:T(128)} %param.11) | copy-start | bytes 580
  12.9 4.7 %copy-start.4 = (f32[128]{0:T(128)S(1)}, f32[128]{0:T(128)}, u32[]{:S(2)}) copy-start(f32[128]{0:T(128)} %param.12) | copy-start | bytes 1540
  12.9 4.8 %copy-start.3 = (bf16[3,48,128]{2,1,0:T(8,128)(2,1)S(1)}, bf16[3,48,128]{2,1,0:T(8,128)(2,1)}, u32[]{:S(2)}) copy-start(bf16[3,48,128]{2,1,0:T(8,128)(2,1)} %param.9) | copy-start | bytes 110596
Sparse Core Ops, SparseCore 0:
  10.1 183.6 all-gather.2
  214.2 91.0 reduce-scatter.1
